TPU v7x, 256 devices: a whole 4x4x8 slice. The times are simulated.
256 devices in a mesh: tok: 16 (over z, core), tp: 16 (over x, y).
Axes of the slice: x: 4, y: 4, z: 8, core: 2. Of those that a mesh axis runs over, the one named last changes fastest.
Arguments:
- hidden_states: bfloat16 [32768, 1024], P(('tok', 'tp')), may hold values from -40 to 40
- first_gain: float32 [1024], replicated, may hold values from 0.1 to 1.9
- second_gain: float32 [1024], replicated, may hold values from 0.1 to 1.9
- w_query: bfloat16 [1024, 1024], P(None, 'tp'), may hold values from -1 to 1
- w_keyval: bfloat16 [1024, 1024], replicated, may hold values from -0.375 to 0.375
- w_out: bfloat16 [1024, 1024], P('tp'), may hold values from -0.75 to 0.75
- kv_cache: bfloat16 [384, 128, 1024], P('tok'), may hold values from -310 to 310
- page_table: int32 [32, 16], P('tok'), may hold values from 0 to 383, as said below
- cached_len: int32 [32], P('tok'), may hold values from 128 to 2048, as said below
- expert_ids: int32 [32768, 8], P(('tok', 'tp')), may hold values from 0 to 31, all different within a row; in each aligned block of 128 rows (0 to 127, 128 to 255, ...) at most 64 rows name the same one
- gate_weights: float32 [32768, 8], P(('tok', 'tp')), may hold values from 0.1 to 1
- w_gate_up: bfloat16 [32, 1024, 1024], P('tp', 'tok'), may hold values from -0.1875 to 0.1875
- w_down: bfloat16 [32, 512, 1024], P('tp', 'tok'), may hold values from -1 to 1
Outputs:
- layer_out: bfloat16 [32768, 1024], P(('tok', 'tp'))
Inputs may be any that keep to these rules, and one draw needn't show every extreme that they name: `page_table`: request r's entries are pages of its own tok index, rows 24 * (r // 2) to 24 * (r // 2 + 1) - 1; its first 8 entries are the same for all requests of that tok index, and all other entries name pages that no other entry names. `cached_len`: some request has exactly 2048 cached tokens. `expert_ids`: in the rows of one device (aligned blocks of 128 rows) no expert is named by more than 64 rows, and a row names 8 different experts.
All inputs are finite; a program needn't handle non-finite values.
Results may differ from a plain program's by a relative error of at most 0.017.
The roundings to bfloat16 on the way count: a program that leaves them out, or rounds other values in their place, can miss the bound.
Values may be sent and summed in bfloat16 or wider, within the bound.
No kernel may reach another device: no remote copies, remote signals or barrier semaphores. Data moves between devices by JAX's collectives and lax.ppermute only.
A program may use at most 128 MiB of HBM per device.

v0:
```python
import jax
import jax.numpy as jnp
from jax import lax
from jax.sharding import PartitionSpec as P

D = 1024
HEADS = 16
KV_HEADS = 8
HEAD_DIM = 64
EXPERTS = 32
FF_EXPERT = 512
TOP = 8
NEW = 1024
MAX_CACHED = 2048
REQ_DEV = 2
ATTN_SCALE = 0.015625
EPSILON = 1e-06
THETA = 10000.0


def rms_norm(values, gain):
    wide = values.astype(jnp.float32)
    factor = lax.rsqrt(jnp.mean(wide * wide, axis=-1, keepdims=True) + EPSILON)
    return (wide * factor * gain).astype(jnp.bfloat16)


def rotate(values, positions):
    row_count = values.shape[0]
    shaped = values.reshape(row_count, -1, HEAD_DIM)
    half_dim = HEAD_DIM // 2
    exponent = jnp.arange(half_dim).astype(jnp.float32) * (2.0 / HEAD_DIM)
    frequency = jnp.power(THETA, -exponent)
    angles = positions.astype(jnp.float32)[:, None] * frequency[None, :]
    cosine = jnp.cos(angles)[:, None, :]
    sine_part = jnp.sin(angles)[:, None, :]
    leading = shaped[..., :half_dim]
    trailing = shaped[..., half_dim:]
    turned = jnp.concatenate(
        [leading * cosine - trailing * sine_part, trailing * cosine + leading * sine_part], axis=-1
    )
    return turned.reshape(row_count, -1)


def attend_request(queries, keys_total, values_total, length):
    block_rows = min(NEW, 512)
    key_index = jnp.arange(MAX_CACHED + NEW, dtype=jnp.int32)

    def one_block(block_start):
        block_query = lax.dynamic_slice_in_dim(queries, block_start, block_rows, 0)
        scores = (
            jnp.einsum(
                "qgpd,kgd->gpqk", block_query, keys_total, preferred_element_type=jnp.float32
            )
            * ATTN_SCALE
        )
        query_pos = block_start + jnp.arange(block_rows, dtype=jnp.int32)
        allowed = jnp.where(
            key_index[None, :] < MAX_CACHED,
            key_index[None, :] < length,
            key_index[None, :] - MAX_CACHED <= query_pos[:, None],
        )
        scores = jnp.where(allowed, scores, -1e30)
        top_score = jnp.max(scores, axis=-1, keepdims=True)
        weights = jnp.exp(scores - top_score)
        probs = (weights / jnp.sum(weights, axis=-1, keepdims=True)).astype(jnp.bfloat16)
        mixed = jnp.einsum(
            "gpqk,kgd->qgpd", probs, values_total, preferred_element_type=jnp.float32
        )
        return mixed.astype(jnp.bfloat16).reshape(block_rows, -1)

    starts = jnp.arange(NEW // block_rows, dtype=jnp.int32) * block_rows
    return lax.map(one_block, starts).reshape(NEW, -1)


def shards(
    hidden_states,
    first_gain,
    second_gain,
    w_query,
    w_keyval,
    w_out,
    kv_cache,
    page_table,
    cached_len,
    expert_ids,
    gate_weights,
    w_gate_up,
    w_down,
):
    gate_up_full, down_full = (
        lax.all_gather(w_gate_up, "tok", axis=1, tiled=True),
        lax.all_gather(w_down, "tok", axis=1, tiled=True),
    )
    tok_rows = hidden_states.shape[0]
    tp_size = lax.axis_size("tp")
    tp_rank = lax.axis_index("tp")
    local_heads = HEADS // tp_size
    group_size = HEADS // KV_HEADS
    local_kv = max(local_heads // group_size, 1)
    per_group = local_heads // local_kv
    head_width = local_heads * HEAD_DIM
    kv_width = local_kv * HEAD_DIM
    kv_cols = KV_HEADS * HEAD_DIM
    group_tokens = REQ_DEV * NEW
    first_kv = tp_rank * local_heads // group_size
    request_range = jnp.arange(REQ_DEV, dtype=jnp.int32)
    normed = rms_norm(hidden_states, first_gain)
    key_part = lax.dynamic_slice_in_dim(w_keyval, first_kv * HEAD_DIM, kv_width, 1)
    value_part = lax.dynamic_slice_in_dim(w_keyval, kv_cols + first_kv * HEAD_DIM, kv_width, 1)
    piece = lax.all_gather(normed, "tp", axis=0, tiled=True)
    row_index = jnp.arange(piece.shape[0], dtype=jnp.int32)
    owner = row_index // NEW
    base_len = jnp.sum(
        jnp.where(owner[:, None] == request_range[None, :], cached_len[None, :], 0), axis=1
    )
    piece_pos = base_len + row_index % NEW
    query_rows = rotate(jnp.dot(piece, w_query, preferred_element_type=jnp.float32), piece_pos)
    key_rows = rotate(jnp.dot(piece, key_part, preferred_element_type=jnp.float32), piece_pos)
    value_rows = jnp.dot(piece, value_part, preferred_element_type=jnp.float32)
    projected = jnp.concatenate([query_rows, key_rows, value_rows], axis=1).astype(jnp.bfloat16)
    queries = projected[:, :head_width].reshape(REQ_DEV, NEW, local_kv, per_group, HEAD_DIM)
    new_keys = projected[:, head_width : head_width + kv_width].reshape(
        REQ_DEV, NEW, local_kv, HEAD_DIM
    )
    new_values = projected[:, head_width + kv_width :].reshape(REQ_DEV, NEW, local_kv, HEAD_DIM)
    cache_keys = lax.dynamic_slice_in_dim(kv_cache, first_kv * HEAD_DIM, kv_width, 2)
    cache_values = lax.dynamic_slice_in_dim(kv_cache, kv_cols + first_kv * HEAD_DIM, kv_width, 2)
    local_pages = page_table - lax.axis_index("tok") * kv_cache.shape[0]

    def per_request(inputs):
        page_ids, length, request_q, request_k, request_v = inputs
        keys_total = jnp.concatenate(
            [
                jnp.take(cache_keys, page_ids, axis=0).reshape(MAX_CACHED, local_kv, HEAD_DIM),
                request_k,
            ],
            axis=0,
        )
        values_total = jnp.concatenate(
            [
                jnp.take(cache_values, page_ids, axis=0).reshape(MAX_CACHED, local_kv, HEAD_DIM),
                request_v,
            ],
            axis=0,
        )
        return attend_request(request_q, keys_total, values_total, length)

    attended = lax.map(
        per_request, (local_pages, cached_len, queries, new_keys, new_values)
    ).reshape(group_tokens, head_width)
    projected_out = lax.psum_scatter(
        jnp.dot(attended, w_out, preferred_element_type=jnp.float32),
        "tp",
        scatter_dimension=0,
        tiled=True,
    )
    middle = (hidden_states.astype(jnp.float32) + projected_out).astype(jnp.bfloat16)
    normed_two = rms_norm(middle, second_gain)
    experts_local = EXPERTS // tp_size
    capacity = 2 * tok_rows * TOP // EXPERTS
    expert_range = jnp.arange(EXPERTS, dtype=jnp.int32)
    onehot = (expert_ids[:, :, None] == expert_range[None, None, :]).astype(jnp.int32)
    per_token = jnp.sum(onehot, axis=1)
    earlier = jnp.cumsum(per_token, axis=0) - per_token
    slot_ids = jnp.sum(onehot * earlier[:, None, :], axis=2)
    target = expert_ids * capacity + slot_ids
    outgoing_rows = jnp.broadcast_to(normed_two[:, None, :], (tok_rows, TOP, D))
    send_buffer = jnp.zeros((EXPERTS * capacity, D), jnp.bfloat16).at[target].set(outgoing_rows)
    received = lax.all_to_all(
        send_buffer.reshape(tp_size, experts_local, capacity, D),
        "tp",
        split_axis=0,
        concat_axis=2,
        tiled=True,
    )
    received = received.reshape(experts_local, tp_size * capacity, D)
    both = jnp.einsum("esd,edf->esf", received, gate_up_full, preferred_element_type=jnp.float32)
    activated = (jax.nn.silu(both[..., :FF_EXPERT]) * both[..., FF_EXPERT:]).astype(jnp.bfloat16)
    produced = jnp.einsum(
        "esf,efd->esd", activated, down_full, preferred_element_type=jnp.float32
    ).astype(jnp.bfloat16)
    returned = lax.all_to_all(
        produced.reshape(experts_local, tp_size, capacity, D),
        "tp",
        split_axis=1,
        concat_axis=0,
        tiled=True,
    )
    returned = returned.reshape(EXPERTS * capacity, D)
    picked = returned[target]
    mixture = jnp.einsum("tk,tkd->td", gate_weights, picked.astype(jnp.float32))
    return (middle.astype(jnp.float32) + mixture).astype(jnp.bfloat16)


def solution(mesh):
    in_specs = (
        P(("tok", "tp"), None),
        P(),
        P(),
        P(None, "tp"),
        P(),
        P("tp", None),
        P("tok", None, None),
        P("tok", None),
        P("tok"),
        P(("tok", "tp"), None),
        P(("tok", "tp"), None),
        P("tp", "tok", None),
        P("tp", "tok", None),
    )
    out_specs = P(("tok", "tp"), None)
    return jax.shard_map(shards, mesh=mesh, in_specs=in_specs, out_specs=out_specs, check_vma=False)
```

profile of v0, /device:TPU:24, one launch (start us, length us, event | category | flops | bytes accessed | tf_op | source)
XLA Modules:
  0.0 391.7 jit_solution(955928082948849221)
XLA Ops:
  7.4 1.2 fusion.29
  8.6 1.8 fusion.31
  10.6 0.7 fusion.55
  11.3 2.8 constant_dynamic-slice_fusion.1
  14.1 55.6 %all-gather.4.cloned.1.call-done = bf16[2048,1024]{1,0:T(8,128)(2,1)} async-done(((bf16[128,1024]{1,0:T(8,128)(2,1)}), bf16[2048,1024]{1,0:T(8,128)(2,1)}) %all-gather.4.cloned.1.call-update) | async-done | bytes 4194320 | tf_op jit(solution)/shard_map/all_gather | solution.py:110
  69.7 3.8 convolution_bitcast_fusion
  73.5 1.4 convolution_bitcast_fusion.1
  74.9 1.2 fusion.50
  76.1 0.8 pad_maximum_fusion.2
  76.9 1.1 reshape.360
  78.0 0.8 copy.43
  78.8 3.7 convolution_convert_fusion.1
  82.8 44.6 %while.34 = (s32[]{:T(128)}, bf16[2,1024,64]{2,1,0:T(8,128)(2,1)}, bf16[2,1024,1,1,64]{1,4,3,2,0:T(8,128)(2,1)}, s32[2,16]{1,0:T(2,128)S(1)}, bf16[24,128,64]{2,...) while((s32[]{:T(128)}, bf16[2,1024,64]{2,1,0:T(8,128)(2,1)}, ...), condition=%wide.region_7.9_spmd, body=%wide.region_2.8_spmd.sunk | while | flops 420259424 | bytes 28236604 | solution.py:148
  82.8 0.6 gather_fusion
  83.5 1.8 gather_fusion.1
  85.9 0.9 dynamic-slice_bitcast_fusion.5
  86.8 0.6 dynamic_slice.94
  87.5 16.5 %while.35 = (s32[]{:T(128)}, bf16[2,512,64]{1,2,0:T(8,128)(2,1)S(1)}, s32[]{:T(128)}, s32[2]{0:T(128)S(1)}, bf16[1024,1,1,64]{0,3,2,1:T(8,128)(2,1)S(1)}, /*inde...) while((s32[]{:T(128)}, ...), condition=%wide.region_6.7_spmd.clone.clone, body=%wide.region_3.6_spmd.clone.clone.sunk | while | flops 418423296 | bytes 19843236 | solution.py:72
  87.5 0.6 dynamic_slice.96
  90.0 0.6 iota_add_fusion.4
  90.6 0.6 iota_compare_fusion.4
  91.3 2.0 fusion.89
  93.3 1.0 fusion.90
  94.3 1.4 fusion.91
  95.7 0.6 dynamic_slice.96
  98.3 0.6 iota_add_fusion.4
  98.9 0.6 iota_compare_fusion.4
  99.6 2.0 fusion.89
  101.5 1.0 fusion.90
  102.5 1.4 fusion.91
  104.2 0.8 copy-done.5
  105.1 0.6 gather_fusion
  105.7 1.8 gather_fusion.1
  108.2 0.9 dynamic-slice_bitcast_fusion.5
  109.1 0.6 dynamic_slice.94
  109.7 16.5 %while.35 = (s32[]{:T(128)}, bf16[2,512,64]{1,2,0:T(8,128)(2,1)S(1)}, s32[]{:T(128)}, s32[2]{0:T(128)S(1)}, bf16[1024,1,1,64]{0,3,2,1:T(8,128)(2,1)S(1)}, /*inde...) while((s32[]{:T(128)}, ...), condition=%wide.region_6.7_spmd.clone.clone, body=%wide.region_3.6_spmd.clone.clone.sunk | while | flops 418423296 | bytes 19843236 | solution.py:72
  109.7 0.6 dynamic_slice.96
  112.3 0.6 iota_add_fusion.4
  112.9 0.6 iota_compare_fusion.4
  113.6 2.0 fusion.89
  115.5 1.0 fusion.90
  116.5 1.4 fusion.91
  118.0 0.6 dynamic_slice.96
  120.5 0.6 iota_add_fusion.4
  121.2 0.6 iota_compare_fusion.4
  121.8 2.0 fusion.89
  123.8 1.0 fusion.90
  124.8 1.4 fusion.91
  126.5 0.8 copy-done.5
  127.3 5.5 %fusion.70 = f32[2048,1024]{1,0:T(8,128)} fusion(bf16[2048,64]{1,0:T(8,128)(2,1)} %bitcast.130, bf16[64,1024]{1,0:T(8,128)(2,1)S(1)} %copy-done.6), kind=kOutput, calls=%fused_computation.117 | convolution fusion | flops 268435456 | bytes 8781824 | tf_op jit(solution)/shard_map/dot_general | solution.py:152
  134.1 89.1 %reduce-scatter.2.cloned.1.call-done = f32[128,1024]{1,0:T(8,128)} async-done(((f32[2048,1024]{1,0:T(8,128)}), f32[128,1024]{1,0:T(8,128)}) %reduce-scatter.2.cloned.1.call-update) | async-done | bytes 524304 | tf_op jit(solution)/shard_map/reduce_scatter | solution.py:151
  223.2 1.2 fusion.33
  224.5 7.9 %scatter_custom_fusion = bf16[2048,1024]{1,0:T(8,128)(2,1)} fusion(s32[1024]{0:T(1024)S(1)} %reshape.399, bf16[]{:T(256)} %constant.161.clone.1, bf16[128,1024]{1,0:T(8,128)(2,1)S(1)} %fusion.35), kind=kCustom, calls=%fused_computation.45 | custom fusion | bytes 4456450 | tf_op jit(solution)/shard_map/scatter | solution.py:168
  232.5 5.6 %all-to-all-start = ((bf16[16,2,64,1024]{3,2,1,0:T(8,128)(2,1)}), bf16[16,2,64,1024]{3,2,1,0:T(8,128)(2,1)}, u32[]{:S(2)}, u32[]{:S(2)}) async-start(bf16[16,2,64,1024]{3,2,1,0:T(8,128)(2,1)} %bitcast.126), calls=%async_computation.1 | async-start | bytes 8388608 | tf_op jit(solution)/shard_map/all_to_all | solution.py:169
  238.7 51.2 %all-to-all-done = bf16[16,2,64,1024]{3,2,1,0:T(8,128)(2,1)} async-done(((bf16[16,2,64,1024]{3,2,1,0:T(8,128)(2,1)}), bf16[16,2,64,1024]{3,2,1,0:T(8,128)(2,1)}, u32[]{:S(2)}, u32[]{:S(2)}) %all-to-all-start) | async-done | bytes 4194336 | tf_op jit(solution)/shard_map/all_to_all | solution.py:169
  289.8 4.8 %copy.50 = bf16[1,2,16,64,1024]{4,3,2,1,0:T(8,128)(2,1)} copy(bf16[1,2,16,64,1024]{4,3,1,2,0:T(8,128)(2,1)} %bitcast.14) | data formatting | bytes 8388608 | tf_op jit(solution)/shard_map/all_to_all | solution.py:169
  294.7 11.2 %fusion.71 = f32[2,1024,1024]{2,1,0:T(8,128)} fusion(bf16[2,1024,1024]{2,1,0:T(8,128)(2,1)} %bitcast.127, bf16[2,1024,1024]{2,1,0:T(8,128)(2,1)} %all-gather.6.cloned.1.call-done), kind=kOutput, calls=%fused_computation.118 | convolution fusion | flops 4294967296 | bytes 16777216 | tf_op jit(solution)/shard_map/esd,edf->esf/dot_general | solution.py:177
  305.9 6.4 %convolution_convert_fusion = bf16[2,1024,1024]{2,1,0:T(8,128)(2,1)S(1)} fusion(bf16[2,512,1024]{2,1,0:T(8,128)(2,1)} %all-gather.8.cloned.1.call-done, f32[2,1024,1024]{2,1,0:T(8,128)} %fusion.71), kind=kOutput, calls=%fused_computation.39 | convolution fusion | flops 2155872256 | bytes 14680064 | tf_op jit(solution)/shard_map/esf,efd->esd/dot_general | solution.py:179
  312.3 2.4 copy.51
  314.7 7.2 %all-to-all-start.1 = ((bf16[2,16,64,1024]{3,2,0,1:T(8,128)(2,1)}), bf16[2,16,64,1024]{3,2,0,1:T(8,128)(2,1)}, u32[]{:S(2)}, u32[]{:S(2)}) async-start(bf16[2,16,64,1024]{3,2,0,1:T(8,128)(2,1)} %copy.51), calls=%async_computation.2 | async-start | bytes 8388608 | tf_op jit(solution)/shard_map/all_to_all | solution.py:182
  322.1 50.2 %all-to-all-done.1 = bf16[2,16,64,1024]{3,2,0,1:T(8,128)(2,1)} async-done(((bf16[2,16,64,1024]{3,2,0,1:T(8,128)(2,1)}), bf16[2,16,64,1024]{3,2,0,1:T(8,128)(2,1)}, u32[]{:S(2)}, u32[]{:S(2)}) %all-to-all-start.1) | async-done | bytes 4194336 | tf_op jit(solution)/shard_map/all_to_all | solution.py:182
  372.3 8.9 %gather_fusion.2 = bf16[1024,1024]{1,0:T(8,128)(2,1)} fusion(bf16[2048,1024]{1,0:T(8,128)(2,1)} %bitcast.19, s32[1024]{0:T(1024)S(1)} %broadcast_clamp_fusion), kind=kCustom, calls=%fused_computation.2 | custom fusion | bytes 4198400 | tf_op jit(solution)/shard_map/gather | solution.py:190
  381.2 2.3 fusion.22
  383.5 0.8 fusion.36
  (88 shorter events, 4.3 us)
Async XLA Ops:
  7.4 62.3 %copy-start = (bf16[1024,1024]{1,0:T(8,128)(2,1)S(1)}, bf16[1024,1024]{1,0:T(8,128)(2,1)}, u32[]{:S(2)}) copy-start(bf16[1024,1024]{1,0:T(8,128)(2,1)} %param.23) | copy-start | bytes 6291460
  7.4 6.7 %copy-start.11 = (s32[2,16]{1,0:T(2,128)S(1)}, s32[2,16]{1,0:T(2,128)}, u32[]{:S(2)}) copy-start(s32[2,16]{1,0:T(2,128)} %param.26) | copy-start | bytes 388
  7.4 62.3 %all-gather.4.cloned.1.call-start = ((), (), s32[]{:S(2)}) async-start(), calls=%async_computation.3 | async-start | bytes 4456448 | tf_op jit(solution)/shard_map/all_gather | solution.py:110
  10.4 212.7 %reduce-scatter.2.cloned.1.call-start = ((), (), s32[]{:S(2)}) async-start(), calls=%async_computation.4 | async-start | bytes 8912896 | tf_op jit(solution)/shard_map/reduce_scatter | solution.py:151
  14.1 59.4 %copy-start.7 = (bf16[1024,64]{0,1:T(8,128)(2,1)S(1)}, bf16[1024,64]{0,1:T(8,128)(2,1)}, u32[]{:S(2)}) copy-start(bf16[1024,64]{0,1:T(8,128)(2,1)} %param.22) | copy-start | bytes 393220
  69.7 3.8 copy-start.2
  78.8 3.9 %copy-start.12 = (s32[2]{0:T(128)S(1)}, s32[2]{0:T(128)}, u32[]{:S(2)}) copy-start(s32[2]{0:T(128)} %param.27) | copy-start | bytes 28
  82.7 44.6 %copy-start.6 = (bf16[64,1024]{1,0:T(8,128)(2,1)S(1)}, bf16[64,1024]{1,0:T(8,128)(2,1)}, u32[]{:S(2)}) copy-start(bf16[64,1024]{1,0:T(8,128)(2,1)} %param.24) | copy-start | bytes 393220
  87.5 16.7 %copy-start.4 = (bf16[2,1024,64]{2,1,0:T(8,128)(2,1)S(1)}, bf16[2,1024,64]{2,1,0:T(8,128)(2,1)}, u32[]{:S(2)}) copy-start(bf16[2,1024,64]{2,1,0:T(8,128)(2,1)} %get-tuple-element.550) | copy-start | bytes 786436 | tf_op jit(solution)/shard_map/while
  104.2 0.8 copy-start.5
  109.7 16.7 %copy-start.4 = (bf16[2,1024,64]{2,1,0:T(8,128)(2,1)S(1)}, bf16[2,1024,64]{2,1,0:T(8,128)(2,1)}, u32[]{:S(2)}) copy-start(bf16[2,1024,64]{2,1,0:T(8,128)(2,1)} %get-tuple-element.550) | copy-start | bytes 786436 | tf_op jit(solution)/shard_map/while
  126.5 0.8 copy-start.5
  132.8 0.7 copy-start.8
  132.8 90.4 %copy-start.3 = (bf16[128,1024]{1,0:T(8,128)(2,1)S(1)}, bf16[128,1024]{1,0:T(8,128)(2,1)}, u32[]{:S(2)}) copy-start(bf16[128,1024]{1,0:T(8,128)(2,1)} %param.19) | copy-start | bytes 786436
  132.8 91.6 %copy-start.9 = (f32[1024]{0:T(1024)S(1)}, f32[1024]{0:T(1024)}, u32[]{:S(2)}) copy-start(f32[1024]{0:T(1024)} %param.21) | copy-start | bytes 12292
  132.8 161.8 %all-gather.6.cloned.1.call-start = ((), (), s32[]{:S(2)}) async-start(), calls=%async_computation.5 | async-start | bytes 4456448 | tf_op jit(solution)/shard_map/all_gather | solution.py:91
  232.5 57.4 %all-to-all-start = ((bf16[16,2,64,1024]{3,2,1,0:T(8,128)(2,1)}), bf16[16,2,64,1024]{3,2,1,0:T(8,128)(2,1)}, u32[]{:S(2)}, u32[]{:S(2)}) async-start(bf16[16,2,64,1024]{3,2,1,0:T(8,128)(2,1)} %bitcast.126), calls=%async_computation.1 | async-start | bytes 8388608 | tf_op jit(solution)/shard_map/all_to_all | solution.py:169
  238.1 67.8 %all-gather.8.cloned.1.call-start = ((), (), s32[]{:S(2)}) async-start(), calls=%async_computation.6 | async-start | bytes 2228224 | tf_op jit(solution)/shard_map/all_gather | solution.py:92
  314.7 7.2 %copy-start.10 = (f32[128,8]{0,1:T(8,128)S(1)}, f32[128,8]{0,1:T(8,128)}, u32[]{:S(2)}) copy-start(f32[128,8]{0,1:T(8,128)} %param.29) | copy-start | bytes 12292
  314.7 57.5 %all-to-all-start.1 = ((bf16[2,16,64,1024]{3,2,0,1:T(8,128)(2,1)}), bf16[2,16,64,1024]{3,2,0,1:T(8,128)(2,1)}, u32[]{:S(2)}, u32[]{:S(2)}) async-start(bf16[2,16,64,1024]{3,2,0,1:T(8,128)(2,1)} %copy.51), calls=%async_computation.2 | async-start | bytes 8388608 | tf_op jit(solution)/shard_map/all_to_all | solution.py:182
  372.3 12.0 %copy-start.1 = (bf16[1024,1024]{1,0:T(8,128)(2,1)S(1)}, bf16[1024,1024]{1,0:T(8,128)(2,1)}, u32[]{:S(2)}) copy-start(bf16[1024,1024]{1,0:T(8,128)(2,1)} %param.23) | copy-start | bytes 6291460
Sparse Core Ops, SparseCore 0:
  10.6 59.0 all-gather.3
  133.0 90.1 reduce-scatter.1
Sparse Core Ops, SparseCore 1:
  135.2 41.6 all-gather.5
  240.4 40.7 all-gather.7
where the time goes:
time: 393 us; the launch traced here: 392 us
  waiting for transfers between devices  247 us (63%)
  matrix products  47.9 us (12%)
  local copies, waits for them, and re-layouts  43 us (11%)
  other arithmetic  17.8 us (5%)
  between operations  15.1 us (4%)
  starting transfers between devices  13.1 us (3%)
  loops' own time  7.97 us (2%)
    reduce_scatter x1, waiting for transfers between devices, shards(): lax.psum_scatter(jnp.dot(attended, w_out, preferred_element_type=jnp.floa...  89.1 us
    all_gather x1, waiting for transfers between devices, shards(): piece = lax.all_gather(normed, 'tp', axis=0, tiled=True)  55.6 us
    all_to_all x1, waiting for transfers between devices, shards(): lax.all_to_all(send_buffer.reshape(tp_size, experts_local, capacity, D),...  51.2 us
    all_to_all x1, waiting for transfers between devices, shards(): lax.all_to_all(produced.reshape(experts_local, tp_size, capacity, D), 'tp...  50.2 us
    dot_general x1, matrix products, shards(): jnp.einsum('esd,edf->esf', received, gate_up_full, preferred_element_type...  11.2 us
    gather x1, local copies, waits for them, and re-layouts, shards(): picked = returned[target]  8.89 us
    scatter x1, local copies, waits for them, and re-layouts, shards(): jnp.zeros((EXPERTS * capacity, D), jnp.bfloat16).at[target]  7.92 us
    dot_general x4, matrix products, one_block(): jnp.einsum('qgpd,kgd->gpqk', block_query, keys_total, preferred_element_t...  7.91 us
  transfers between devices with their start and end apart: 6, of which 4 were waited for; matrix products, arithmetic and copies ran while one was open for 8% of the time, Pallas kernels for 0%

commit v1 on v0

--- a/solution.py
+++ b/solution.py
@@ -2,6 +2,7 @@
 import jax.numpy as jnp
 from jax import lax
 from jax.sharding import PartitionSpec as P
+from jax.lax import all_to_all, psum
 
 D = 1024
 HEADS = 16
@@ -107,7 +108,9 @@
     normed = rms_norm(hidden_states, first_gain)
     key_part = lax.dynamic_slice_in_dim(w_keyval, first_kv * HEAD_DIM, kv_width, 1)
     value_part = lax.dynamic_slice_in_dim(w_keyval, kv_cols + first_kv * HEAD_DIM, kv_width, 1)
-    piece = lax.all_gather(normed, "tp", axis=0, tiled=True)
+    piece = jnp.concatenate(
+        all_to_all(jnp.stack([normed for _ in range(psum(1, "tp"))], axis=0), "tp", 0, 0), axis=0
+    )
     row_index = jnp.arange(piece.shape[0], dtype=jnp.int32)
     owner = row_index // NEW
     base_len = jnp.sum(

time: 393 us -> 411 us (1.046)
  waiting for transfers between devices: 247 us -> 257 us
  starting transfers between devices: 13.1 us -> 20.5 us
    all_gather x1 -> x0, waiting for transfers between devices: 55.6 us -> none  [shards(): piece = lax.all_gather(normed, 'tp', axis=0, tiled=True)]
    all_to_all x0 -> x1, waiting for transfers between devices: none -> 52.6 us  [shards(): all_to_all(jnp.stack([normed for _ in range(psum(1, 'tp'))], axis=0), 'tp...]
    reduce_scatter x1, waiting for transfers between devices: 89.1 us -> 102 us  [shards(): lax.psum_scatter(jnp.dot(attended, w_out, preferred_element_type=jnp.floa...]
    all_to_all x0 -> x1, starting transfers between devices: none -> 7.3 us  [shards(): all_to_all(jnp.stack([normed for _ in range(psum(1, 'tp'))], axis=0), 'tp...]
  transfers between devices with their start and end apart: 6 -> 6, of which waited for: 4 -> 4; matrix products, arithmetic and copies ran while one was open for 8% -> 7% of each run, Pallas kernels for 0% -> 0%
where the time goes in v1:
time: 411 us; the launch traced here: 410 us
  waiting for transfers between devices  257 us (63%)
  matrix products  50 us (12%)
  local copies, waits for them, and re-layouts  44.5 us (11%)
  starting transfers between devices  20.5 us (5%)
  other arithmetic  15.7 us (4%)
  between operations  15.1 us (4%)
  loops' own time  8.03 us (2%)
    reduce_scatter x1, waiting for transfers between devices, shards(): lax.psum_scatter(jnp.dot(attended, w_out, preferred_element_type=jnp.floa...  102 us
    all_to_all x1, waiting for transfers between devices, shards(): all_to_all(jnp.stack([normed for _ in range(psum(1, 'tp'))], axis=0), 'tp...  52.6 us
    all_to_all x1, waiting for transfers between devices, shards(): lax.all_to_all(send_buffer.reshape(tp_size, experts_local, capacity, D),...  51 us
    all_to_all x1, waiting for transfers between devices, shards(): lax.all_to_all(produced.reshape(experts_local, tp_size, capacity, D), 'tp...  50.1 us
    dot_general x1, matrix products, shards(): jnp.einsum('esd,edf->esf', received, gate_up_full, preferred_element_type...  11.2 us
    gather x1, local copies, waits for them, and re-layouts, shards(): picked = returned[target]  8.9 us
  transfers between devices with their start and end apart: 6, of which 4 were waited for; matrix products, arithmetic and copies ran while one was open for 7% of the time, Pallas kernels for 0%

profile of v1, /device:TPU:24, one launch (start us, length us, event | category | flops | bytes accessed | tf_op | source)
XLA Modules:
  0.0 410.4 jit_solution(3162848735946489916)
XLA Ops:
  7.4 1.2 fusion.29
  8.6 1.1 fusion.31
  9.7 2.5 stack.2
  12.2 7.3 %all-to-all-start = ((bf16[16,128,1024]{2,1,0:T(8,128)(2,1)}), bf16[16,128,1024]{2,1,0:T(8,128)(2,1)}, u32[]{:S(2)}, u32[]{:S(2)}) async-start(bf16[16,128,1024]{2,1,0:T(8,128)(2,1)} %stack.2), calls=%async_computation | async-start | bytes 8388608 | tf_op jit(solution)/shard_map/all_to_all | solution.py:112
  19.7 2.8 constant_dynamic-slice_fusion.1
  22.6 52.6 %all-to-all-done = bf16[16,128,1024]{2,1,0:T(8,128)(2,1)} async-done(((bf16[16,128,1024]{2,1,0:T(8,128)(2,1)}), bf16[16,128,1024]{2,1,0:T(8,128)(2,1)}, u32[]{:S(2)}, u32[]{:S(2)}) %all-to-all-start) | async-done | bytes 4194336 | tf_op jit(solution)/shard_map/all_to_all | solution.py:112
  75.2 3.6 convolution_bitcast_fusion
  78.9 3.7 convolution_convert_fusion.1
  82.6 3.6 convolution_bitcast_fusion.1
  86.2 1.2 fusion.50
  87.6 0.8 copy.43
  88.7 44.5 %while.34 = (s32[]{:T(128)}, bf16[2,1024,64]{2,1,0:T(8,128)(2,1)}, bf16[2,1024,1,1,64]{1,4,3,2,0:T(8,128)(2,1)}, s32[2,16]{1,0:T(2,128)S(1)}, bf16[24,128,64]{2,...) while((s32[]{:T(128)}, bf16[2,1024,64]{2,1,0:T(8,128)(2,1)}, ...), condition=%wide.region_7.9_spmd, body=%wide.region_2.8_spmd.sunk | while | flops 420259424 | bytes 28236604 | solution.py:151
  88.7 0.6 gather_fusion
  89.4 1.8 gather_fusion.1
  91.8 0.9 dynamic-slice_bitcast_fusion.5
  92.7 0.6 dynamic_slice.94
  93.4 16.5 %while.35 = (s32[]{:T(128)}, bf16[2,512,64]{1,2,0:T(8,128)(2,1)S(1)}, s32[]{:T(128)}, s32[2]{0:T(128)S(1)}, bf16[1024,1,1,64]{0,3,2,1:T(8,128)(2,1)S(1)}, /*inde...) while((s32[]{:T(128)}, ...), condition=%wide.region_6.7_spmd.clone.clone, body=%wide.region_3.6_spmd.clone.clone.sunk | while | flops 418423296 | bytes 19843236 | solution.py:73
  93.4 0.6 dynamic_slice.96
  95.9 0.6 iota_add_fusion.4
  96.6 0.6 iota_compare_fusion.4
  97.2 2.0 fusion.89
  99.2 1.0 fusion.90
  100.2 1.4 fusion.91
  101.7 0.6 dynamic_slice.96
  104.2 0.6 iota_add_fusion.4
  104.8 0.6 iota_compare_fusion.4
  105.5 2.0 fusion.89
  107.4 1.0 fusion.90
  108.4 1.4 fusion.91
  110.1 0.8 copy-done.4
  111.0 0.6 gather_fusion
  111.6 1.8 gather_fusion.1
  114.1 0.9 dynamic-slice_bitcast_fusion.5
  115.0 0.6 dynamic_slice.94
  115.6 16.5 %while.35 = (s32[]{:T(128)}, bf16[2,512,64]{1,2,0:T(8,128)(2,1)S(1)}, s32[]{:T(128)}, s32[2]{0:T(128)S(1)}, bf16[1024,1,1,64]{0,3,2,1:T(8,128)(2,1)S(1)}, /*inde...) while((s32[]{:T(128)}, ...), condition=%wide.region_6.7_spmd.clone.clone, body=%wide.region_3.6_spmd.clone.clone.sunk | while | flops 418423296 | bytes 19843236 | solution.py:73
  115.6 0.6 dynamic_slice.96
  118.2 0.6 iota_add_fusion.4
  118.8 0.6 iota_compare_fusion.4
  119.4 2.0 fusion.89
  121.4 1.0 fusion.90
  122.4 1.4 fusion.91
  123.9 0.6 dynamic_slice.96
  126.4 0.6 iota_add_fusion.4
  127.0 0.6 iota_compare_fusion.4
  127.7 2.0 fusion.89
  129.7 1.0 fusion.90
  130.7 1.4 fusion.91
  132.4 0.8 copy-done.4
  133.2 5.5 %fusion.70 = f32[2048,1024]{1,0:T(8,128)} fusion(bf16[2048,64]{1,0:T(8,128)(2,1)} %bitcast.131, bf16[64,1024]{1,0:T(8,128)(2,1)S(1)} %copy-done.5), kind=kOutput, calls=%fused_computation.117 | convolution fusion | flops 268435456 | bytes 8781824 | tf_op jit(solution)/shard_map/dot_general | solution.py:155
  140.0 101.9 %reduce-scatter.2.cloned.1.call-done = f32[128,1024]{1,0:T(8,128)} async-done(((f32[2048,1024]{1,0:T(8,128)}), f32[128,1024]{1,0:T(8,128)}) %reduce-scatter.2.cloned.1.call-update) | async-done | bytes 524304 | tf_op jit(solution)/shard_map/reduce_scatter | solution.py:154
  241.9 1.2 fusion.33
  243.3 7.9 %scatter_custom_fusion = bf16[2048,1024]{1,0:T(8,128)(2,1)} fusion(s32[1024]{0:T(1024)S(1)} %reshape.405, bf16[]{:T(256)} %constant.161.clone.1, bf16[128,1024]{1,0:T(8,128)(2,1)S(1)} %fusion.35), kind=kCustom, calls=%fused_computation.45 | custom fusion | bytes 4456450 | tf_op jit(solution)/shard_map/scatter | solution.py:171
  251.2 5.7 %all-to-all-start.1 = ((bf16[16,2,64,1024]{3,2,1,0:T(8,128)(2,1)}), bf16[16,2,64,1024]{3,2,1,0:T(8,128)(2,1)}, u32[]{:S(2)}, u32[]{:S(2)}) async-start(bf16[16,2,64,1024]{3,2,1,0:T(8,128)(2,1)} %bitcast.127), calls=%async_computation.2 | async-start | bytes 8388608 | tf_op jit(solution)/shard_map/all_to_all | solution.py:172
  256.9 0.5 all-gather.5.cloned.1.call-update
  257.5 51.0 %all-to-all-done.1 = bf16[16,2,64,1024]{3,2,1,0:T(8,128)(2,1)} async-done(((bf16[16,2,64,1024]{3,2,1,0:T(8,128)(2,1)}), bf16[16,2,64,1024]{3,2,1,0:T(8,128)(2,1)}, u32[]{:S(2)}, u32[]{:S(2)}) %all-to-all-start.1) | async-done | bytes 4194336 | tf_op jit(solution)/shard_map/all_to_all | solution.py:172
  308.5 4.8 %copy.50 = bf16[1,2,16,64,1024]{4,3,2,1,0:T(8,128)(2,1)} copy(bf16[1,2,16,64,1024]{4,3,1,2,0:T(8,128)(2,1)} %bitcast.15) | data formatting | bytes 8388608 | tf_op jit(solution)/shard_map/all_to_all | solution.py:172
  313.3 11.2 %fusion.71 = f32[2,1024,1024]{2,1,0:T(8,128)} fusion(bf16[2,1024,1024]{2,1,0:T(8,128)(2,1)} %bitcast.128, bf16[2,1024,1024]{2,1,0:T(8,128)(2,1)} %all-gather.3.cloned.1.call-done), kind=kOutput, calls=%fused_computation.118 | convolution fusion | flops 4294967296 | bytes 16777216 | tf_op jit(solution)/shard_map/esd,edf->esf/dot_general | solution.py:180
  324.5 6.4 %convolution_convert_fusion = bf16[2,1024,1024]{2,1,0:T(8,128)(2,1)S(1)} fusion(bf16[2,512,1024]{2,1,0:T(8,128)(2,1)} %all-gather.5.cloned.1.call-done, f32[2,1024,1024]{2,1,0:T(8,128)} %fusion.71), kind=kOutput, calls=%fused_computation.39 | convolution fusion | flops 2155872256 | bytes 14680064 | tf_op jit(solution)/shard_map/esf,efd->esd/dot_general | solution.py:182
  330.9 2.4 copy.51
  333.4 7.3 %all-to-all-start.2 = ((bf16[2,16,64,1024]{3,2,0,1:T(8,128)(2,1)}), bf16[2,16,64,1024]{3,2,0,1:T(8,128)(2,1)}, u32[]{:S(2)}, u32[]{:S(2)}) async-start(bf16[2,16,64,1024]{3,2,0,1:T(8,128)(2,1)} %copy.51), calls=%async_computation.3 | async-start | bytes 8388608 | tf_op jit(solution)/shard_map/all_to_all | solution.py:185
  340.8 50.1 %all-to-all-done.2 = bf16[2,16,64,1024]{3,2,0,1:T(8,128)(2,1)} async-done(((bf16[2,16,64,1024]{3,2,0,1:T(8,128)(2,1)}), bf16[2,16,64,1024]{3,2,0,1:T(8,128)(2,1)}, u32[]{:S(2)}, u32[]{:S(2)}) %all-to-all-start.2) | async-done | bytes 4194336 | tf_op jit(solution)/shard_map/all_to_all | solution.py:185
  390.9 8.9 %gather_fusion.2 = bf16[1024,1024]{1,0:T(8,128)(2,1)} fusion(bf16[2048,1024]{1,0:T(8,128)(2,1)} %bitcast.20, s32[1024]{0:T(1024)S(1)} %broadcast_clamp_fusion), kind=kCustom, calls=%fused_computation.2 | custom fusion | bytes 4198400 | tf_op jit(solution)/shard_map/gather | solution.py:193
  399.8 2.3 fusion.22
  402.1 0.8 fusion.36
  (86 shorter events, 4.0 us)
Async XLA Ops:
  7.4 67.9 %copy-start = (bf16[1024,1024]{1,0:T(8,128)(2,1)S(1)}, bf16[1024,1024]{1,0:T(8,128)(2,1)}, u32[]{:S(2)}) copy-start(bf16[1024,1024]{1,0:T(8,128)(2,1)} %param.23) | copy-start | bytes 6291460
  12.2 7.4 %copy-start.11 = (s32[2]{0:T(128)S(1)}, s32[2]{0:T(128)}, u32[]{:S(2)}) copy-start(s32[2]{0:T(128)} %param.27) | copy-start | bytes 28
  12.2 10.4 %copy-start.10 = (s32[2,16]{1,0:T(2,128)S(1)}, s32[2,16]{1,0:T(2,128)}, u32[]{:S(2)}) copy-start(s32[2,16]{1,0:T(2,128)} %param.26) | copy-start | bytes 388
  12.2 63.0 %all-to-all-start = ((bf16[16,128,1024]{2,1,0:T(8,128)(2,1)}), bf16[16,128,1024]{2,1,0:T(8,128)(2,1)}, u32[]{:S(2)}, u32[]{:S(2)}) async-start(bf16[16,128,1024]{2,1,0:T(8,128)(2,1)} %stack.2), calls=%async_computation | async-start | bytes 8388608 | tf_op jit(solution)/shard_map/all_to_all | solution.py:112
  19.5 222.4 %reduce-scatter.2.cloned.1.call-start = ((), (), s32[]{:S(2)}) async-start(), calls=%async_computation.4 | async-start | bytes 8912896 | tf_op jit(solution)/shard_map/reduce_scatter | solution.py:154
  78.9 3.7 copy-start.6
  88.6 44.5 %copy-start.5 = (bf16[64,1024]{1,0:T(8,128)(2,1)S(1)}, bf16[64,1024]{1,0:T(8,128)(2,1)}, u32[]{:S(2)}) copy-start(bf16[64,1024]{1,0:T(8,128)(2,1)} %param.24) | copy-start | bytes 393220
  93.4 16.7 %copy-start.3 = (bf16[2,1024,64]{2,1,0:T(8,128)(2,1)S(1)}, bf16[2,1024,64]{2,1,0:T(8,128)(2,1)}, u32[]{:S(2)}) copy-start(bf16[2,1024,64]{2,1,0:T(8,128)(2,1)} %get-tuple-element.550) | copy-start | bytes 786436 | tf_op jit(solution)/shard_map/while
  110.1 0.8 copy-start.4
  115.6 16.7 %copy-start.3 = (bf16[2,1024,64]{2,1,0:T(8,128)(2,1)S(1)}, bf16[2,1024,64]{2,1,0:T(8,128)(2,1)}, u32[]{:S(2)}) copy-start(bf16[2,1024,64]{2,1,0:T(8,128)(2,1)} %get-tuple-element.550) | copy-start | bytes 786436 | tf_op jit(solution)/shard_map/while
  132.4 0.8 copy-start.4
  138.7 0.7 copy-start.7
  138.7 103.2 %copy-start.2 = (bf16[128,1024]{1,0:T(8,128)(2,1)S(1)}, bf16[128,1024]{1,0:T(8,128)(2,1)}, u32[]{:S(2)}) copy-start(bf16[128,1024]{1,0:T(8,128)(2,1)} %param.19) | copy-start | bytes 786436
  138.7 104.4 %copy-start.8 = (f32[1024]{0:T(1024)S(1)}, f32[1024]{0:T(1024)}, u32[]{:S(2)}) copy-start(f32[1024]{0:T(1024)} %param.21) | copy-start | bytes 12292
  138.7 174.6 %all-gather.3.cloned.1.call-start = ((), (), s32[]{:S(2)}) async-start(), calls=%async_computation.5 | async-start | bytes 4456448 | tf_op jit(solution)/shard_map/all_gather | solution.py:92
  251.2 57.3 %all-to-all-start.1 = ((bf16[16,2,64,1024]{3,2,1,0:T(8,128)(2,1)}), bf16[16,2,64,1024]{3,2,1,0:T(8,128)(2,1)}, u32[]{:S(2)}, u32[]{:S(2)}) async-start(bf16[16,2,64,1024]{3,2,1,0:T(8,128)(2,1)} %bitcast.127), calls=%async_computation.2 | async-start | bytes 8388608 | tf_op jit(solution)/shard_map/all_to_all | solution.py:172
  256.9 67.6 %all-gather.5.cloned.1.call-start = ((), (), s32[]{:S(2)}) async-start(), calls=%async_computation.6 | async-start | bytes 2228224 | tf_op jit(solution)/shard_map/all_gather | solution.py:93
  333.4 7.3 %copy-start.9 = (f32[128,8]{0,1:T(8,128)S(1)}, f32[128,8]{0,1:T(8,128)}, u32[]{:S(2)}) copy-start(f32[128,8]{0,1:T(8,128)} %param.29) | copy-start | bytes 12292
  333.4 57.6 %all-to-all-start.2 = ((bf16[2,16,64,1024]{3,2,0,1:T(8,128)(2,1)}), bf16[2,16,64,1024]{3,2,0,1:T(8,128)(2,1)}, u32[]{:S(2)}, u32[]{:S(2)}) async-start(bf16[2,16,64,1024]{3,2,0,1:T(8,128)(2,1)} %copy.51), calls=%async_computation.3 | async-start | bytes 8388608 | tf_op jit(solution)/shard_map/all_to_all | solution.py:185
  390.9 12.0 %copy-start.1 = (bf16[1024,1024]{1,0:T(8,128)(2,1)S(1)}, bf16[1024,1024]{1,0:T(8,128)(2,1)}, u32[]{:S(2)}) copy-start(bf16[1024,1024]{1,0:T(8,128)(2,1)} %param.23) | copy-start | bytes 6291460
Sparse Core Ops, SparseCore 0:
  138.8 103.0 reduce-scatter.1
Sparse Core Ops, SparseCore 1:
  141.0 54.8 all-gather.2
  259.2 40.8 all-gather.4
